TPU v7x, 256 devices: a whole 4x4x8 slice. The times are simulated.
256 devices in a mesh: frame: 32 (over z, x_hi, core), head: 8 (over y, x_lo).
Axes of the slice: x: 4 (x_hi: 2, x_lo: 2; x = x_hi * 2 + x_lo), y: 4, z: 8, core: 2. Of those that a mesh axis runs over, the one named last changes fastest.
Arguments:
- query_vectors: bfloat16 [12288, 3072], P('frame', 'head'), may hold values from -17 to 17
- key_vectors: bfloat16 [12288, 3072], P('frame', 'head'), may hold values from -6 to 6
- value_vectors: bfloat16 [12288, 3072], P('frame', 'head'), may hold values from -6 to 6
- tile_mask: int32 [96, 96], replicated, may hold values from 0 to 1, as said below
- out_weight: bfloat16 [3072, 3072], P('head'), may hold values from -0.109375 to 0.109375
Outputs:
- projected: bfloat16 [12288, 3072], P(('frame', 'head'))
Inputs may be any that keep to these rules, and one draw needn't show every extreme that they name: The slab holds packed clips of whole tiles. Each clip lays its tiles out in order on a grid of latent frames by tile rows by tile columns. One clip spans 72 tiles and its latent frame holds 48 tiles, in 4 or 8 columns; every other clip has 2 to 4 rows and 2 to 4 columns, by clip. tile_mask[a, b] is 1 exactly when tiles a and b lie in the same clip and their frame, row and column indices each differ by at most 1.
All inputs are finite; a program needn't handle non-finite values.
Results may differ from a plain program's by a relative error of at most 0.02.
Values may be sent and summed in bfloat16 or wider, within the bound.
No kernel may reach another device: no remote copies, remote signals or barrier semaphores. Data moves between devices by JAX's collectives and lax.ppermute only.
A program may use at most 128 MiB of HBM per device.

v0:
```python
import math
import jax
import jax.numpy as jnp
from jax import lax
from jax.sharding import PartitionSpec as P

HD = 128
TILE = 128
NEGATIVE = -1e30


def expand_mask(tile_block, row_count, col_count):
    query_tiles, key_tiles = tile_block.shape
    tile_rows = row_count // query_tiles
    expanded = jnp.broadcast_to(
        tile_block[:, None, :, None], (query_tiles, tile_rows, key_tiles, tile_rows)
    )
    return expanded.reshape(row_count, col_count) > 0


def block_scores(query_block, key_block, allowed):
    head_count = query_block.shape[1] // HD
    query_heads = query_block.reshape(query_block.shape[0], head_count, HD)
    key_heads = key_block.reshape(key_block.shape[0], head_count, HD)
    raw_scores = jnp.einsum(
        "qhd,khd->hqk", query_heads, key_heads, preferred_element_type=jnp.float32
    ) * (1.0 / math.sqrt(HD))
    return jnp.where(allowed[None], raw_scores, NEGATIVE)


def online_update(running, key_block, value_block, allowed, query_block):
    numerator, row_top, totals = running
    scores = block_scores(query_block, key_block, allowed)
    new_top = jnp.maximum(row_top, jnp.max(scores, axis=2, keepdims=True))
    weights = jnp.where(allowed[None], jnp.exp(scores - new_top), 0.0)
    factor = jnp.exp(row_top - new_top)
    totals = totals * factor + jnp.sum(weights, axis=2, keepdims=True)
    value_heads = value_block.reshape(value_block.shape[0], row_top.shape[0], HD)
    numerator = numerator * factor + jnp.einsum(
        "hqk,khd->hqd",
        weights.astype(jnp.bfloat16),
        value_heads,
        preferred_element_type=jnp.float32,
    )
    return (numerator, new_top, totals)


def shards(query_vectors, key_vectors, value_vectors, tile_mask, out_weight):
    row_count = query_vectors.shape[0]
    channels = query_vectors.shape[1]
    head_count = channels // HD
    frame_pos = lax.axis_index("frame")
    tiles_here = row_count // TILE
    query_tiles = lax.dynamic_slice_in_dim(tile_mask, frame_pos * tiles_here, tiles_here, 0)
    initial = (
        jnp.zeros((head_count, row_count, HD), jnp.float32),
        jnp.full((head_count, row_count, 1), NEGATIVE, jnp.float32),
        jnp.zeros((head_count, row_count, 1), jnp.float32),
    )
    key_piece = lax.all_gather(key_vectors, "frame", axis=0, tiled=True)
    value_piece = lax.all_gather(value_vectors, "frame", axis=0, tiled=True)
    length = key_piece.shape[0]
    block_rows = 2 * row_count
    block_span = length // block_rows
    key_tiles = query_tiles
    key_tiles = key_tiles.reshape(tiles_here, block_span, block_rows // TILE).transpose(1, 0, 2)
    key_blocks = key_piece.reshape(block_span, block_rows, channels)
    value_blocks = value_piece.reshape(block_span, block_rows, channels)

    def advance(current, element):
        key_block, value_block, tile_block = element
        allowed = expand_mask(tile_block, row_count, block_rows)
        return (online_update(current, key_block, value_block, allowed, query_vectors), None)

    result, _ = lax.scan(advance, initial, (key_blocks, value_blocks, key_tiles))
    numerator, row_top, totals = result
    attended = (
        (numerator / totals).transpose(1, 0, 2).reshape(row_count, channels).astype(jnp.bfloat16)
    )
    return lax.psum_scatter(
        jnp.dot(attended, out_weight, preferred_element_type=jnp.float32).astype(jnp.bfloat16),
        "head",
        scatter_dimension=0,
        tiled=True,
    )


def solution(mesh):
    in_specs = (P("frame", "head"), P("frame", "head"), P("frame", "head"), P(), P("head", None))
    out_specs = P(("frame", "head"), None)
    return jax.shard_map(shards, mesh=mesh, in_specs=in_specs, out_specs=out_specs, check_vma=False)
```

profile of v0, /device:TPU:1, one launch (start us, length us, event | category | flops | bytes accessed | tf_op | source)
XLA Modules:
  0.0 568.9 jit_solution(12067339337692195843)
XLA Ops:
  11.3 107.8 %all-gather.3.cloned.1.call-done = bf16[12288,384]{1,0:T(8,128)(2,1)} async-done(((bf16[384,384]{1,0:T(8,128)(2,1)}), bf16[12288,384]{1,0:T(8,128)(2,1)}) %all-gather.3.cloned.1.call-update) | async-done | bytes 9437200 | tf_op jit(solution)/shard_map/all_gather | solution.py:60
  119.1 104.5 %all-gather.5.cloned.1.call-done = bf16[12288,384]{1,0:T(8,128)(2,1)} async-done(((bf16[384,384]{1,0:T(8,128)(2,1)}), bf16[12288,384]{1,0:T(8,128)(2,1)}) %all-gather.5.cloned.1.call-update) | async-done | bytes 9437200 | tf_op jit(solution)/shard_map/all_gather | solution.py:61
  223.6 278.3 %while.15 = (s32[]{:T(128)}, f32[3,384,128]{2,1,0:T(8,128)}, f32[3,384,1]{1,0,2:T(4,128)S(1)}, f32[3,384,1]{1,0,2:T(4,128)S(1)}, s32[16,3,6]{2,0,1:T(8,128)}, /*...) while((s32[]{:T(128)}, f32[3,384,128]{2,1,0:T(8,128)}, ...), condition=%wide.region_3.4_spmd.clone, body=%wide.region_0.3_spmd.clone.sunk | while | flops 464935680 | bytes 22782352 | solution.py:75
  223.6 2.4 constant_dynamic-slice_fusion.6
  228.8 3.7 fusion.33
  232.5 3.0 fusion.36
  236.6 4.3 fusion.35
  240.8 2.4 constant_dynamic-slice_fusion.6
  246.0 3.7 fusion.33
  249.7 3.0 fusion.36
  253.8 4.5 fusion.35
  258.2 2.4 constant_dynamic-slice_fusion.6
  263.4 3.7 fusion.33
  267.1 3.0 fusion.36
  271.2 4.5 fusion.35
  275.7 2.4 constant_dynamic-slice_fusion.6
  280.8 3.7 fusion.33
  284.5 3.0 fusion.36
  288.6 4.5 fusion.35
  293.1 2.4 constant_dynamic-slice_fusion.6
  298.2 3.7 fusion.33
  301.9 3.0 fusion.36
  306.0 4.5 fusion.35
  310.5 2.4 constant_dynamic-slice_fusion.6
  315.7 3.7 fusion.33
  319.3 3.0 fusion.36
  323.4 4.5 fusion.35
  327.9 2.4 constant_dynamic-slice_fusion.6
  333.1 3.7 fusion.33
  336.7 3.0 fusion.36
  340.8 4.5 fusion.35
  345.3 2.4 constant_dynamic-slice_fusion.6
  350.5 3.7 fusion.33
  354.1 3.0 fusion.36
  358.2 4.5 fusion.35
  367.9 3.7 fusion.33
  371.5 3.0 fusion.36
  375.6 4.5 fusion.35
  385.3 3.7 fusion.33
  388.9 3.0 fusion.36
  393.0 4.5 fusion.35
  397.5 2.4 constant_dynamic-slice_fusion.6
  402.7 3.7 fusion.33
  406.3 3.0 fusion.36
  410.4 4.5 fusion.35
  414.9 2.4 constant_dynamic-slice_fusion.6
  420.1 3.7 fusion.33
  423.8 3.0 fusion.36
  427.8 4.5 fusion.35
  437.5 3.7 fusion.33
  441.2 3.0 fusion.36
  445.2 4.5 fusion.35
  454.9 3.7 fusion.33
  458.6 3.0 fusion.36
  462.7 4.5 fusion.35
  467.1 2.4 constant_dynamic-slice_fusion.6
  472.3 3.7 fusion.33
  476.0 3.0 fusion.36
  480.1 4.5 fusion.35
  489.7 3.7 fusion.33
  493.4 3.0 fusion.36
  497.5 4.5 fusion.35
  503.3 2.8 convolution_convert_fusion
  506.2 56.2 %reduce-scatter.2.cloned.1.call-done = bf16[48,3072]{1,0:T(8,128)(2,1)} async-done(((bf16[384,3072]{1,0:T(8,128)(2,1)}), bf16[48,3072]{1,0:T(8,128)(2,1)}) %reduce-scatter.2.cloned.1.call-update) | async-done | bytes 294928 | tf_op jit(solution)/shard_map/reduce_scatter | solution.py:80
  (213 shorter events, 81.0 us)
Async XLA Ops:
  6.5 496.8 %copy-start = (bf16[384,3072]{1,0:T(8,128)(2,1)S(1)}, bf16[384,3072]{1,0:T(8,128)(2,1)}, u32[]{:S(2)}) copy-start(bf16[384,3072]{1,0:T(8,128)(2,1)} %param.11) | copy-start | bytes 7077892
  6.5 112.6 %all-gather.3.cloned.1.call-start = ((), (), s32[]{:S(2)}) async-start(), calls=%async_computation.1 | async-start | bytes 9732096 | tf_op jit(solution)/shard_map/all_gather | solution.py:60
  7.3 216.4 %all-gather.5.cloned.1.call-start = ((), (), s32[]{:S(2)}) async-start(), calls=%async_computation.2 | async-start | bytes 9732096 | tf_op jit(solution)/shard_map/all_gather | solution.py:61
  8.0 554.4 %reduce-scatter.2.cloned.1.call-start = ((), (), s32[]{:S(2)}) async-start(), calls=%async_computation.3 | async-start | bytes 2654208 | tf_op jit(solution)/shard_map/reduce_scatter | solution.py:80
  232.5 3.0 copy-start.1
  249.7 3.0 copy-start.1
  267.1 3.0 copy-start.1
  284.5 3.0 copy-start.1
  301.9 3.0 copy-start.1
  319.3 3.0 copy-start.1
  336.7 3.0 copy-start.1
  354.1 3.0 copy-start.1
  371.5 3.0 copy-start.1
  388.9 3.0 copy-start.1
  406.3 3.0 copy-start.1
  423.7 3.0 copy-start.1
  441.1 3.0 copy-start.1
  458.6 3.0 copy-start.1
  476.0 3.0 copy-start.1
  493.4 3.0 copy-start.1
Sparse Core Ops, SparseCore 0:
  10.1 108.9 all-gather.2
  121.9 101.6 all-gather.4
  506.3 56.0 reduce-scatter.1
where the time goes:
time: 572 us; the launch traced here: 569 us
  waiting for transfers between devices  270 us (47%)
  matrix products  132 us (23%)
  local copies, waits for them, and re-layouts  105 us (18%)
  other arithmetic  47.9 us (8%)
  between operations  13.2 us (2%)
    all_gather x1, waiting for transfers between devices, shards(): key_piece = lax.all_gather(key_vectors, 'frame', axis=0, tiled=True)  108 us
    all_gather x1, waiting for transfers between devices, shards(): value_piece = lax.all_gather(value_vectors, 'frame', axis=0, tiled=True)  104 us
    dynamic_slice x64, local copies, waits for them, and re-layouts, shards(): lax.scan(advance, initial, (key_blocks, value_blocks, key_tiles))  87.7 us
    dot_general x16, matrix products, online_update(): jnp.einsum('hqk,khd->hqd', weights.astype(jnp.bfloat16), value_heads, pre...  71.2 us
    dot_general x16, matrix products, block_scores(): jnp.einsum('qhd,khd->hqk', query_heads, key_heads, preferred_element_type...  58.4 us
    reduce_scatter x1, waiting for transfers between devices, shards(): lax.psum_scatter(jnp.dot(attended, out_weight, preferred_element_type=jnp...  56.2 us
    reduce_sum x16, other arithmetic, online_update(): totals = totals * factor + jnp.sum(weights, axis=2, keepdims=True)  47.3 us
  transfers between devices with their start and end apart: 3, of which 3 were waited for; matrix products, arithmetic and copies ran while one was open for 1% of the time, Pallas kernels for 0%

commit v1 on v0

--- a/solution.py
+++ b/solution.py
@@ -58,7 +58,9 @@
         jnp.zeros((head_count, row_count, 1), jnp.float32),
     )
     key_piece = lax.all_gather(key_vectors, "frame", axis=0, tiled=True)
-    value_piece = lax.all_gather(value_vectors, "frame", axis=0, tiled=True)
+    value_piece = jnp.concatenate(
+        lax.all_to_all(jnp.stack([value_vectors] * lax.axis_size("frame")), "frame", 0, 0), axis=0
+    )
     length = key_piece.shape[0]
     block_rows = 2 * row_count
     block_span = length // block_rows

time: 572 us -> 616 us (1.077)
  waiting for transfers between devices: 270 us -> 296 us
  starting transfers between devices: 0.08 us -> 12.8 us
    all_to_all x0 -> x1, waiting for transfers between devices: none -> 235 us  [shards(): lax.all_to_all(jnp.stack([value_vectors] * lax.axis_size('frame')), 'fram...]
    all_gather x1, waiting for transfers between devices: 108 us -> 0.01 us  [shards(): key_piece = lax.all_gather(key_vectors, 'frame', axis=0, tiled=True)]
    all_gather x1 -> x0, waiting for transfers between devices: 104 us -> none  [shards(): value_piece = lax.all_gather(value_vectors, 'frame', axis=0, tiled=True)]
    all_to_all x0 -> x1, starting transfers between devices: none -> 12.8 us  [shards(): lax.all_to_all(jnp.stack([value_vectors] * lax.axis_size('frame')), 'fram...]
    another operation x0 -> x1, local copies, waits for them, and re-layouts: none -> 6.25 us  [shards(): jnp.stack([value_vectors] * lax.axis_size('frame'))]
  transfers between devices with their start and end apart: 3 -> 3, of which waited for: 3 -> 2; matrix products, arithmetic and copies ran while one was open for 1% -> 0% of each run, Pallas kernels for 0% -> 0%
where the time goes in v1:
time: 616 us; the launch traced here: 613 us
  waiting for transfers between devices  296 us (48%)
  matrix products  132 us (21%)
  local copies, waits for them, and re-layouts  110 us (18%)
  other arithmetic  47.9 us (8%)
  between operations  13.5 us (2%)
  starting transfers between devices  12.8 us (2%)
    all_to_all x1, waiting for transfers between devices, shards(): lax.all_to_all(jnp.stack([value_vectors] * lax.axis_size('frame')), 'fram...  235 us
    dynamic_slice x64, local copies, waits for them, and re-layouts, shards(): lax.scan(advance, initial, (key_blocks, value_blocks, key_tiles))  88 us
    dot_general x16, matrix products, online_update(): jnp.einsum('hqk,khd->hqd', weights.astype(jnp.bfloat16), value_heads, pre...  70.9 us
    reduce_scatter x1, waiting for transfers between devices, shards(): lax.psum_scatter(jnp.dot(attended, out_weight, preferred_element_type=jnp...  60.7 us
    dot_general x16, matrix products, block_scores(): jnp.einsum('qhd,khd->hqk', query_heads, key_heads, preferred_element_type...  58.4 us
    reduce_sum x16, other arithmetic, online_update(): totals = totals * factor + jnp.sum(weights, axis=2, keepdims=True)  47.3 us
    all_to_all x1, starting transfers between devices, shards(): lax.all_to_all(jnp.stack([value_vectors] * lax.axis_size('frame')), 'fram...  12.8 us
  transfers between devices with their start and end apart: 3, of which 2 were waited for; matrix products, arithmetic and copies ran while one was open for 0% of the time, Pallas kernels for 0%

profile of v1, /device:TPU:1, one launch (start us, length us, event | category | flops | bytes accessed | tf_op | source)
XLA Modules:
  0.0 613.4 jit_solution(17997110552082791891)
XLA Ops:
  6.5 6.3 %stack.2 = bf16[32,384,384]{2,1,0:T(8,128)(2,1)} broadcast(bf16[384,384]{1,0:T(8,128)(2,1)} %param.9), dimensions={1,2} | broadcast | bytes 9732096 | tf_op jit(solution)/shard_map/stack | solution.py:62
  12.8 12.8 %all-to-all-start = ((bf16[32,384,384]{2,1,0:T(8,128)(2,1)}), bf16[32,384,384]{2,1,0:T(8,128)(2,1)}, u32[]{:S(2)}, u32[]{:S(2)}) async-start(bf16[32,384,384]{2,1,0:T(8,128)(2,1)} %stack.2), calls=%async_computation | async-start | bytes 18874368 | tf_op jit(solution)/shard_map/all_to_all | solution.py:62
  28.7 234.6 %all-to-all-done = bf16[32,384,384]{2,1,0:T(8,128)(2,1)} async-done(((bf16[32,384,384]{2,1,0:T(8,128)(2,1)}), bf16[32,384,384]{2,1,0:T(8,128)(2,1)}, u32[]{:S(2)}, u32[]{:S(2)}) %all-to-all-start) | async-done | bytes 9437216 | tf_op jit(solution)/shard_map/all_to_all | solution.py:62
  263.2 278.4 %while.15 = (s32[]{:T(128)}, f32[3,384,128]{2,1,0:T(8,128)}, f32[3,384,1]{1,0,2:T(4,128)S(1)}, f32[3,384,1]{1,0,2:T(4,128)S(1)}, s32[16,3,6]{2,0,1:T(8,128)}, /*...) while((s32[]{:T(128)}, f32[3,384,128]{2,1,0:T(8,128)}, ...), condition=%wide.region_3.4_spmd.clone, body=%wide.region_0.3_spmd.clone.sunk | while | flops 464935680 | bytes 22782352 | solution.py:77
  263.2 2.4 constant_dynamic-slice_fusion.6
  268.5 3.7 fusion.33
  272.1 3.0 fusion.36
  276.2 4.3 fusion.35
  280.5 2.4 constant_dynamic-slice_fusion.6
  285.7 3.7 fusion.33
  289.4 3.0 fusion.36
  293.4 4.4 fusion.35
  297.9 2.4 constant_dynamic-slice_fusion.6
  303.1 3.7 fusion.33
  306.8 3.0 fusion.36
  310.8 4.4 fusion.35
  315.3 2.4 constant_dynamic-slice_fusion.6
  320.5 3.7 fusion.33
  324.2 3.0 fusion.36
  328.3 4.4 fusion.35
  337.9 3.7 fusion.33
  341.6 3.0 fusion.36
  345.7 4.4 fusion.35
  355.3 3.7 fusion.33
  359.0 3.0 fusion.36
  363.1 4.4 fusion.35
  367.5 2.4 constant_dynamic-slice_fusion.6
  372.7 3.7 fusion.33
  376.4 3.0 fusion.36
  380.5 4.4 fusion.35
  384.9 2.4 constant_dynamic-slice_fusion.6
  390.1 3.7 fusion.33
  393.8 3.0 fusion.36
  397.9 4.4 fusion.35
  402.3 2.4 constant_dynamic-slice_fusion.6
  407.6 3.7 fusion.33
  411.2 3.0 fusion.36
  415.3 4.4 fusion.35
  425.0 3.7 fusion.33
  428.6 3.0 fusion.36
  432.7 4.4 fusion.35
  442.4 3.7 fusion.33
  446.0 3.0 fusion.36
  450.1 4.4 fusion.35
  454.6 2.4 constant_dynamic-slice_fusion.6
  459.8 3.7 fusion.33
  463.4 3.0 fusion.36
  467.5 4.4 fusion.35
  472.0 2.4 constant_dynamic-slice_fusion.6
  477.2 3.7 fusion.33
  480.9 3.0 fusion.36
  484.9 4.4 fusion.35
  489.4 2.4 constant_dynamic-slice_fusion.6
  494.6 3.7 fusion.33
  498.3 3.0 fusion.36
  502.3 4.4 fusion.35
  512.0 3.7 fusion.33
  515.7 3.0 fusion.36
  519.7 4.4 fusion.35
  529.4 3.7 fusion.33
  533.1 3.0 fusion.36
  537.2 4.4 fusion.35
  543.0 2.8 convolution_convert_fusion
  545.8 60.7 %reduce-scatter.2.cloned.1.call-done = bf16[48,3072]{1,0:T(8,128)(2,1)} async-done(((bf16[384,3072]{1,0:T(8,128)(2,1)}), bf16[48,3072]{1,0:T(8,128)(2,1)}) %reduce-scatter.2.cloned.1.call-update) | async-done | bytes 294928 | tf_op jit(solution)/shard_map/reduce_scatter | solution.py:82
  (215 shorter events, 81.7 us)
Async XLA Ops:
  6.5 536.4 %copy-start = (bf16[384,3072]{1,0:T(8,128)(2,1)S(1)}, bf16[384,3072]{1,0:T(8,128)(2,1)}, u32[]{:S(2)}) copy-start(bf16[384,3072]{1,0:T(8,128)(2,1)} %param.11) | copy-start | bytes 7077892
  12.8 15.0 %copy-start.2 = (bf16[384,384]{1,0:T(8,128)(2,1)S(1)}, bf16[384,384]{1,0:T(8,128)(2,1)}, u32[]{:S(2)}) copy-start(bf16[384,384]{1,0:T(8,128)(2,1)} %param.7) | copy-start | bytes 884740
  12.8 250.4 %all-to-all-start = ((bf16[32,384,384]{2,1,0:T(8,128)(2,1)}), bf16[32,384,384]{2,1,0:T(8,128)(2,1)}, u32[]{:S(2)}, u32[]{:S(2)}) async-start(bf16[32,384,384]{2,1,0:T(8,128)(2,1)} %stack.2), calls=%async_computation | async-start | bytes 18874368 | tf_op jit(solution)/shard_map/all_to_all | solution.py:62
  25.6 237.7 %all-gather.2.cloned.1.call-start = ((), (), s32[]{:S(2)}) async-start(), calls=%async_computation.2 | async-start | bytes 9732096 | tf_op jit(solution)/shard_map/all_gather | solution.py:60
  26.3 580.2 %reduce-scatter.2.cloned.1.call-start = ((), (), s32[]{:S(2)}) async-start(), calls=%async_computation.3 | async-start | bytes 2654208 | tf_op jit(solution)/shard_map/reduce_scatter | solution.py:82
  272.1 3.0 copy-start.1
  289.3 3.0 copy-start.1
  306.8 3.0 copy-start.1
  324.2 3.0 copy-start.1
  341.6 3.0 copy-start.1
  359.0 3.0 copy-start.1
  376.4 3.0 copy-start.1
  393.8 3.0 copy-start.1
  411.2 3.0 copy-start.1
  428.6 3.0 copy-start.1
  446.0 3.0 copy-start.1
  463.4 3.0 copy-start.1
  480.8 3.0 copy-start.1
  498.2 3.0 copy-start.1
  515.7 3.0 copy-start.1
  533.1 3.0 copy-start.1
Sparse Core Ops, SparseCore 0:
  29.1 180.5 all-gather.1
  545.9 60.5 reduce-scatter.1
